TPU v7x, 256 devices: a whole 4x4x8 slice. The times are simulated.
256 devices in a mesh: seq: 8 (over z), exp: 8 (over x, y_hi), img: 4 (over y_lo, core).
Axes of the slice: x: 4, y: 4 (y_hi: 2, y_lo: 2; y = y_hi * 2 + y_lo), z: 8, core: 2. Of those that a mesh axis runs over, the one named last changes fastest.
Arguments:
- projected: bfloat16 [32, 1024, 3, 1280], P(('img', 'exp'), 'seq'), parts along dimension 0, may hold values from -6 to 6
- residual: bfloat16 [32, 1024, 1280], P(('img', 'exp'), 'seq'), parts along dimension 0, may hold values from -6 to 6
- attn_proj: bfloat16 [1280, 1280], P('seq'), may hold values from -0.15625 to 0.15625
- norm_gain: float32 [1280], replicated, may hold values from 0.5 to 2
- norm_bias: float32 [1280], replicated, may hold values from -3 to 3
- expert_ids: int32 [32, 1024, 1], P(('img', 'exp')), parts along dimension 0, may hold values from 0 to 15; in each aligned block of 128 rows (0 to 127, 128 to 255, ..., all dimensions but the last counted through in order) at most 12 rows name the same one
- expert_up: bfloat16 [16, 1280, 5120], P('exp', None, 'seq'), may hold values from -0.15625 to 0.15625
- expert_down: bfloat16 [16, 5120, 1280], P('exp', 'seq'), may hold values from -0.078125 to 0.078125
Outputs:
- layer_out: bfloat16 [32, 1024, 1280], P(('img', 'exp'), 'seq'), parts along dimension 0
There are 4 independent parts, one for each index of `img`. A program takes and returns all parts, laid end to end along the dimension named above; an argument that names none is the same for every part. Nothing has to cross between parts.
Inputs may be any that keep to these rules, and one draw needn't show every extreme that they name: `expert_ids`: in each sequence, within every aligned block of 128 tokens, no expert is named by more than 12 tokens.
All inputs are finite; a program needn't handle non-finite values.
Results may differ from a plain program's by a relative error of at most 0.015.
Values may be sent and summed in bfloat16 or wider, within the bound.
No kernel may reach another device: no remote copies, remote signals or barrier semaphores. Data moves between devices by JAX's collectives and lax.ppermute only.
A program may use at most 64 MiB of HBM per device.

v0:
```python
import jax
import jax.numpy as jnp
from jax import lax
from jax.sharding import PartitionSpec as P

HEADS = 16
HEAD_DIM = 80


def attend(gathered):
    queries = gathered[0]
    keys_all = gathered[1]
    values = gathered[2]
    factor = 1.0 / queries.shape[2] ** 0.5
    scores = (
        jnp.einsum("ahdb,chde->habce", queries, keys_all, preferred_element_type=jnp.float32)
        * factor
    )
    peak = jnp.max(scores, axis=(3, 4), keepdims=True)
    powers = jnp.exp(scores - peak)
    weights = (powers * (1.0 / jnp.sum(powers, axis=(3, 4), keepdims=True))).astype(jnp.bfloat16)
    mixed = jnp.einsum("habce,chde->abhd", weights, values, preferred_element_type=jnp.float32)
    return mixed.astype(jnp.bfloat16)


def layer_norm(stream, norm_gain, norm_bias):
    values = stream.astype(jnp.float32)
    centre = jnp.mean(values, axis=-1, keepdims=True)
    centered = values - centre
    variance = jnp.mean(centered * centered, axis=-1, keepdims=True)
    return (centered * lax.rsqrt(variance + 1e-06) * norm_gain + norm_bias).astype(jnp.bfloat16)


def per_device(
    projected, residual, attn_proj, norm_gain, norm_bias, expert_ids, expert_up, expert_down
):
    tok_rows = projected.shape[1]
    model_width = projected.shape[3]
    seq_count = lax.axis_size("seq")
    exp_count = lax.axis_size("exp")
    local_experts = expert_up.shape[0]
    experts = local_experts * exp_count
    cap_dev = 3 * tok_rows // (2 * experts)
    capacity = cap_dev * seq_count
    length = tok_rows * seq_count
    heads_here = HEADS // seq_count
    head_width = heads_here * HEAD_DIM
    token_minor = jnp.transpose(projected[0], (1, 2, 0)).reshape(3, seq_count, head_width, tok_rows)
    arrived_heads = lax.all_to_all(token_minor, "seq", split_axis=1, concat_axis=1, tiled=True)
    attended = attend(arrived_heads.reshape(3, seq_count, heads_here, HEAD_DIM, tok_rows))
    attended = attended.reshape(seq_count, tok_rows, 1, head_width)
    token_heads = lax.all_to_all(attended, "seq", split_axis=0, concat_axis=2, tiled=True).reshape(
        tok_rows, model_width
    )
    projected_sum = jnp.dot(
        token_heads,
        lax.all_gather(attn_proj, "seq", axis=0, tiled=True),
        preferred_element_type=jnp.float32,
    )
    stream_own = residual[0].astype(jnp.float32) + projected_sum
    stream = stream_own.astype(jnp.bfloat16)
    stream_own = stream.astype(jnp.float32)
    normed = layer_norm(stream, norm_gain, norm_bias)
    seq_index = lax.axis_index("seq")
    ids_own = lax.dynamic_slice_in_dim(expert_ids[0, :, 0], seq_index * tok_rows, tok_rows)
    onehot = (ids_own[:, None] == jnp.arange(experts, dtype=jnp.int32)[None, :]).astype(jnp.int32)
    before = jnp.cumsum(onehot, axis=0) - onehot
    order_in_block = jnp.sum(before * onehot, axis=1)
    dest = ids_own * cap_dev + order_in_block
    select = (
        (dest[:, None] == jnp.arange(experts * cap_dev, dtype=jnp.int32)[None, :])
        .astype(jnp.bfloat16)
        .reshape(tok_rows, exp_count, local_experts, cap_dev)
    )
    dispatch = jnp.einsum(
        "tgjc,td->gjcd", select, normed, preferred_element_type=jnp.float32
    ).astype(jnp.bfloat16)
    arrived = lax.all_to_all(dispatch, "exp", split_axis=0, concat_axis=0, tiled=True)
    gathered = lax.all_gather(arrived, "seq", axis=0, tiled=False)
    pieces = []
    for local in range(local_experts):
        lifted = jnp.einsum(
            "secd,df->secf",
            gathered[:, :, local],
            expert_up[local],
            preferred_element_type=jnp.float32,
        )
        hidden = (0.5 * lifted * (1.0 + lax.erf(lifted * 0.5**0.5))).astype(jnp.bfloat16)
        hidden = lax.optimization_barrier(hidden)
        piece = jnp.einsum(
            "secf,fd->secd", hidden, expert_down[local], preferred_element_type=jnp.float32
        )
        pieces.append(piece.astype(jnp.bfloat16))
    pieces = jnp.stack(pieces, axis=2)
    summed = lax.psum_scatter(pieces, "seq", scatter_dimension=0, tiled=True)[0]
    returned = lax.all_to_all(summed, "exp", split_axis=0, concat_axis=0, tiled=True)
    expert_out = jnp.einsum("tgjc,gjcd->td", select, returned, preferred_element_type=jnp.float32)
    return (stream_own + expert_out).astype(jnp.bfloat16)[None]


def solution(mesh):
    return jax.shard_map(
        per_device,
        mesh=mesh,
        in_specs=(
            P(("img", "exp"), "seq", None, None),
            P(("img", "exp"), "seq", None),
            P("seq", None),
            P(),
            P(),
            P(("img", "exp"), None, None),
            P("exp", None, "seq"),
            P("exp", "seq", None),
        ),
        out_specs=P(("img", "exp"), "seq", None),
        check_vma=False,
    )
```

profile of v0, /device:TPU:8, one launch (start us, length us, event | category | flops | bytes accessed | tf_op | source)
XLA Modules:
  0.0 244.4 jit_solution(5946868216613501484)
XLA Ops:
  6.5 0.0 all-gather.4.cloned.1.call-start
  6.5 0.7 all-gather.4.cloned.1.call-update
  7.3 1.6 copy.22
  8.9 1.0 copy.23
  9.9 8.5 %all-to-all-start = ((bf16[3,8,160,128]{3,2,0,1:T(8,128)(2,1)}), bf16[3,8,160,128]{3,2,0,1:T(8,128)(2,1)S(1)}, u32[]{:S(2)}, u32[]{:S(2)}) async-start(bf16[3,8,160,128]{3,2,0,1:T(8,128)(2,1)} %copy.23), calls=%async_computation | async-start | bytes 1966080 | tf_op jit(solution)/shard_map/all_to_all | solution.py:49
  18.4 0.7 dynamic-slice_bitcast_fusion
  19.0 36.1 %all-to-all-done = bf16[3,8,160,128]{3,2,0,1:T(8,128)(2,1)S(1)} async-done(((bf16[3,8,160,128]{3,2,0,1:T(8,128)(2,1)}), bf16[3,8,160,128]{3,2,0,1:T(8,128)(2,1)S(1)}, u32[]{:S(2)}, u32[]{:S(2)}) %all-to-all-start) | async-done | bytes 983072 | tf_op jit(solution)/shard_map/all_to_all | solution.py:49
  55.1 0.1 fusion.45
  55.2 1.3 multiply_reduce_fusion
  56.5 1.4 fusion
  57.9 0.0 copy-start
  57.9 1.8 fusion.25
  59.7 0.0 copy-start.2
  59.7 0.7 copy.31
  60.5 3.4 %all-to-all-start.1 = ((bf16[8,128,1,160]{1,3,2,0:T(8,128)(2,1)}), bf16[8,128,1,160]{1,3,2,0:T(8,128)(2,1)S(1)}, u32[]{:S(2)}, u32[]{:S(2)}) async-start(bf16[8,128,1,160]{1,3,2,0:T(8,128)(2,1)} %bitcast.13), calls=%async_computation.1 | async-start | bytes 655360 | tf_op jit(solution)/shard_map/all_to_all | solution.py:52
  63.9 0.0 all-gather.6.cloned.1.call-start
  64.0 0.1 fusion.43
  64.1 0.2 reduce_window_sum.11
  64.2 0.2 select_reduce_fusion
  64.4 0.7 multiply_add_fusion.1
  65.1 16.4 %all-to-all-done.1 = bf16[8,128,1,160]{1,3,2,0:T(8,128)(2,1)S(1)} async-done(((bf16[8,128,1,160]{1,3,2,0:T(8,128)(2,1)}), bf16[8,128,1,160]{1,3,2,0:T(8,128)(2,1)S(1)}, u32[]{:S(2)}, u32[]{:S(2)}) %all-to-all-start.1) | async-done | bytes 327712 | tf_op jit(solution)/shard_map/all_to_all | solution.py:52
  81.5 0.0 all-gather.4.cloned.1.call-done
  81.5 0.0 copy-done
  81.5 2.6 %fusion.46 = (f32[128]{0:T(128)S(1)}, f32[128,1280]{1,0:T(8,128)S(1)}) fusion(bf16[128,1280]{0,1:T(8,128)(2,1)S(1)} %bitcast.114, bf16[1280,1280]{1,0:T(8,128)(2,1)} %all-gather.4.cloned.1.call-done, bf16[1,128,1280]{2,1,0:T(8,128)(2,1)S(1)} %copy-done), kind=kOutput, calls=%fused_computation.64 | convolution fusion | flops 420249472 | bytes 4588032 | tf_op jit(solution)/shard_map/dot_general | solution.py:55
  84.1 0.2 multiply_reduce_fusion.1
  84.4 0.0 copy-done.1
  84.4 0.0 copy-done.2
  84.4 0.4 convolution_convert_fusion.2
  84.8 0.4 copy.32
  85.2 16.5 %all_to_all.30 = bf16[8,2,12,1280]{3,1,2,0:T(2,128)(2,1)} all-to-all(bf16[8,2,12,1280]{3,1,2,0:T(2,128)(2,1)S(1)} %copy.32), channel_id=1, replica_groups=mesh['seq'=8,'exp'=8,'img'=4] {'exp'}, dimensions={0} | all-to-all | bytes 983040 | tf_op jit(solution)/shard_map/all_to_all | solution.py:78
  101.7 0.0 all-gather.6.cloned.1.call-update
  101.7 0.2 reduce-scatter.2.cloned.1.call-start
  101.9 48.6 %all-gather.6.cloned.1.call-done = bf16[64,2,12,1280]{3,1,2,0:T(2,128)(2,1)} async-done(((bf16[8,2,12,1280]{3,1,2,0:T(2,128)(2,1)}), bf16[64,2,12,1280]{3,1,2,0:T(2,128)(2,1)}) %all-gather.6.cloned.1.call-update) | async-done | bytes 3932176 | tf_op jit(solution)/shard_map/all_gather | solution.py:79
  150.5 3.0 %copy.33 = bf16[64,2,12,1280]{3,2,0,1:T(8,128)(2,1)S(1)} copy(bf16[64,2,12,1280]{3,1,2,0:T(2,128)(2,1)} %all-gather.6.cloned.1.call-done) | data formatting | bytes 7864320 | tf_op jit(solution)/shard_map/all_gather | solution.py:79
  153.5 0.1 copy-done.3
  153.6 2.4 multiply_convert_fusion.3
  156.1 0.0 copy-start.4
  156.1 2.4 multiply_convert_fusion.2
  158.5 0.0 copy-done.4
  158.5 2.2 fusion.2
  160.8 2.2 fusion.3
  163.0 0.7 pad_maximum_fusion
  163.7 3.4 %copy.34 = bf16[8,8,2,12,1280]{4,1,3,2,0:T(8,128)(2,1)} copy(bf16[8,8,2,12,1280]{4,3,1,0,2:T(8,128)(2,1)S(1)} %pad_maximum_fusion) | data formatting | bytes 7864320 | tf_op jit(solution)/shard_map/stack | solution.py:94
  167.1 0.0 reduce-scatter.2.cloned.1.call-update
  167.1 51.6 %reduce-scatter.2.cloned.1.call-done = bf16[1,8,2,12,1280]{4,1,3,2,0:T(8,128)(2,1)} async-done(((bf16[8,8,2,12,1280]{4,1,3,2,0:T(8,128)(2,1)}), bf16[1,8,2,12,1280]{4,1,3,2,0:T(8,128)(2,1)}) %reduce-scatter.2.cloned.1.call-update) | async-done | bytes 491536 | tf_op jit(solution)/shard_map/reduce_scatter | solution.py:95
  218.7 1.5 copy.35
  220.2 16.5 %all_to_all.31 = bf16[8,2,12,1280]{3,1,2,0:T(2,128)(2,1)S(1)} all-to-all(bf16[8,2,12,1280]{3,1,2,0:T(2,128)(2,1)S(1)} %copy.35), channel_id=1, replica_groups=mesh['seq'=8,'exp'=8,'img'=4] {'exp'}, dimensions={0} | all-to-all | bytes 983040 | tf_op jit(solution)/shard_map/all_to_all | solution.py:96
  236.7 1.1 fusion.10
  (6 shorter events, 0.0 us)
Async XLA Ops:
  6.5 74.9 %all-gather.4.cloned.1.call-start = ((), (), s32[]{:S(2)}) async-start(), calls=%async_computation.5 | async-start | bytes 3686400 | tf_op jit(solution)/shard_map/all_gather | solution.py:57
  9.9 45.2 %all-to-all-start = ((bf16[3,8,160,128]{3,2,0,1:T(8,128)(2,1)}), bf16[3,8,160,128]{3,2,0,1:T(8,128)(2,1)S(1)}, u32[]{:S(2)}, u32[]{:S(2)}) async-start(bf16[3,8,160,128]{3,2,0,1:T(8,128)(2,1)} %copy.23), calls=%async_computation | async-start | bytes 1966080 | tf_op jit(solution)/shard_map/all_to_all | solution.py:49
  57.9 23.6 %copy-start = (bf16[1,128,1280]{2,1,0:T(8,128)(2,1)S(1)}, bf16[1,128,1280]{2,1,0:T(8,128)(2,1)}, u32[]{:S(2)}) copy-start(bf16[1,128,1280]{2,1,0:T(8,128)(2,1)} %param.9) | copy-start | bytes 983044
  59.7 24.7 %copy-start.1 = (f32[1280]{0:T(1024)S(1)}, f32[1280]{0:T(1024)}, u32[]{:S(2)}) copy-start(f32[1280]{0:T(1024)} %param.12) | copy-start | bytes 15364
  59.7 24.7 %copy-start.2 = (f32[1280]{0:T(1024)S(1)}, f32[1280]{0:T(1024)}, u32[]{:S(2)}) copy-start(f32[1280]{0:T(1024)} %param.11) | copy-start | bytes 15364
  60.5 21.0 %all-to-all-start.1 = ((bf16[8,128,1,160]{1,3,2,0:T(8,128)(2,1)}), bf16[8,128,1,160]{1,3,2,0:T(8,128)(2,1)S(1)}, u32[]{:S(2)}, u32[]{:S(2)}) async-start(bf16[8,128,1,160]{1,3,2,0:T(8,128)(2,1)} %bitcast.13), calls=%async_computation.1 | async-start | bytes 655360 | tf_op jit(solution)/shard_map/all_to_all | solution.py:52
  63.9 86.6 %all-gather.6.cloned.1.call-start = ((), (), s32[]{:S(2)}) async-start(), calls=%async_computation.7 | async-start | bytes 4423680 | tf_op jit(solution)/shard_map/all_gather | solution.py:79
  101.7 117.0 %reduce-scatter.2.cloned.1.call-start = ((), (), s32[]{:S(2)}) async-start(), calls=%async_computation.6 | async-start | bytes 4423680 | tf_op jit(solution)/shard_map/reduce_scatter | solution.py:95
  150.5 3.1 %copy-start.3 = (bf16[2,1280,640]{2,1,0:T(8,128)(2,1)S(1)}, bf16[2,1280,640]{2,1,0:T(8,128)(2,1)}, u32[]{:S(2)}) copy-start(bf16[2,1280,640]{2,1,0:T(8,128)(2,1)} %param.14) | copy-start | bytes 9830404
  156.1 2.5 %copy-start.4 = (bf16[2,640,1280]{2,1,0:T(8,128)(2,1)S(1)}, bf16[2,640,1280]{2,1,0:T(8,128)(2,1)}, u32[]{:S(2)}) copy-start(bf16[2,640,1280]{2,1,0:T(8,128)(2,1)} %param.15) | copy-start | bytes 9830404
Sparse Core Ops, SparseCore 0:
  9.1 71.9 all-gather.3
  101.8 48.6 all-gather.5
  167.2 51.4 reduce-scatter.1
where the time goes:
time: 245 us; the launch traced here: 244 us
  waiting for transfers between devices  153 us (62%)
  blocking collectives  32.9 us (13%)
  matrix products  16.6 us (7%)
  between operations  13.3 us (5%)
  local copies, waits for them, and re-layouts  12.5 us (5%)
  starting transfers between devices  12.2 us (5%)
  other arithmetic  3.42 us (1%)
    reduce_scatter x1, waiting for transfers between devices, per_device(): summed = lax.psum_scatter(pieces, 'seq', scatter_dimension=0, tiled=True)[0]  51.6 us
    all_gather x1, waiting for transfers between devices, per_device(): gathered = lax.all_gather(arrived, 'seq', axis=0, tiled=False)  48.6 us
    all_to_all x1, waiting for transfers between devices, per_device(): lax.all_to_all(token_minor, 'seq', split_axis=1, concat_axis=1, tiled=True)  36.1 us
    all_to_all x1, blocking collectives, per_device(): lax.all_to_all(summed, 'exp', split_axis=0, concat_axis=0, tiled=True)  16.5 us
    all_to_all x1, blocking collectives, per_device(): lax.all_to_all(dispatch, 'exp', split_axis=0, concat_axis=0, tiled=True)  16.5 us
    all_to_all x1, waiting for transfers between devices, per_device(): lax.all_to_all(attended, 'seq', split_axis=0, concat_axis=2, tiled=True)  16.4 us
    all_to_all x1, starting transfers between devices, per_device(): lax.all_to_all(token_minor, 'seq', split_axis=1, concat_axis=1, tiled=True)  8.47 us
  transfers between devices with their start and end apart: 5, of which 4 were waited for; matrix products, arithmetic and copies ran while one was open for 4% of the time, Pallas kernels for 0%

commit v1 on v0

--- a/solution.py
+++ b/solution.py
@@ -1,3 +1,4 @@
+import functools
 import jax
 import jax.numpy as jnp
 from jax import lax
@@ -5,6 +6,17 @@
 
 HEADS = 16
 HEAD_DIM = 80
+
+
+def link_grid(z, row_axis):
+    left_arr = lax.axis_size(row_axis)
+    reached = jnp.split(z, left_arr, axis=0)
+    out_arr = jnp.stack(reached)
+    block_next = lax.all_to_all(out_arr, row_axis, 0, 0)
+    return jnp.concatenate(block_next, 2)
+
+
+answer_face = functools.partial(link_grid, row_axis="seq")
 
 
 def attend(gathered):
@@ -49,9 +61,7 @@
     arrived_heads = lax.all_to_all(token_minor, "seq", split_axis=1, concat_axis=1, tiled=True)
     attended = attend(arrived_heads.reshape(3, seq_count, heads_here, HEAD_DIM, tok_rows))
     attended = attended.reshape(seq_count, tok_rows, 1, head_width)
-    token_heads = lax.all_to_all(attended, "seq", split_axis=0, concat_axis=2, tiled=True).reshape(
-        tok_rows, model_width
-    )
+    token_heads = answer_face(attended).reshape(tok_rows, model_width)
     projected_sum = jnp.dot(
         token_heads,
         lax.all_gather(attn_proj, "seq", axis=0, tiled=True),

time: 245 us -> 244 us (level)
  waiting for transfers between devices: 153 us -> 148 us
  local copies, waits for them, and re-layouts: 12.5 us -> 16.8 us
    unnamed x11 -> x18, local copies, waits for them, and re-layouts: 1.72 us -> 6.06 us
    all_gather x1, waiting for transfers between devices: 48.6 us -> 45.5 us  [per_device(): gathered = lax.all_gather(arrived, 'seq', axis=0, tiled=False)]
  transfers between devices with their start and end apart: 5 -> 5, of which waited for: 4 -> 4; matrix products, arithmetic and copies ran while one was open for 4% -> 6% of each run, Pallas kernels for 0% -> 0%
where the time goes in v1:
time: 244 us
  waiting for transfers between devices  148 us (61%)
  blocking collectives  33.4 us (14%)
  local copies, waits for them, and re-layouts  16.8 us (7%)
  matrix products  16.6 us (7%)
  between operations  13.3 us (5%)
  starting transfers between devices  12.2 us (5%)
  other arithmetic  3.42 us (1%)
    reduce_scatter x1, waiting for transfers between devices, per_device(): summed = lax.psum_scatter(pieces, 'seq', scatter_dimension=0, tiled=True)[0]  51.6 us
    all_gather x1, waiting for transfers between devices, per_device(): gathered = lax.all_gather(arrived, 'seq', axis=0, tiled=False)  45.5 us
    all_to_all x1, waiting for transfers between devices, per_device(): lax.all_to_all(token_minor, 'seq', split_axis=1, concat_axis=1, tiled=True)  36.1 us
    all_to_all x1, blocking collectives, per_device(): lax.all_to_all(dispatch, 'exp', split_axis=0, concat_axis=0, tiled=True)  16.9 us
    all_to_all x1, blocking collectives, per_device(): lax.all_to_all(summed, 'exp', split_axis=0, concat_axis=0, tiled=True)  16.5 us
    all_to_all x1, waiting for transfers between devices, link_grid(): block_next = lax.all_to_all(out_arr, row_axis, 0, 0)  14.1 us
    all_to_all x1, starting transfers between devices, per_device(): lax.all_to_all(token_minor, 'seq', split_axis=1, concat_axis=1, tiled=True)  8.47 us
    unnamed x18, local copies, waits for them, and re-layouts  6.06 us
  transfers between devices with their start and end apart: 5, of which 4 were waited for; matrix products, arithmetic and copies ran while one was open for 6% of the time, Pallas kernels for 0%

profile of v1, /device:TPU:8, one launch (start us, length us, event | category | flops | bytes accessed | tf_op | source)
XLA Modules:
  0.0 243.6 jit_solution(9458520055724460635)
XLA Ops:
  6.5 0.7 all-gather.4.cloned.1.call-update
  7.3 1.6 copy.21
  8.9 1.0 copy.22
  9.9 8.5 %all-to-all-start = ((bf16[3,8,160,128]{3,2,0,1:T(8,128)(2,1)}), bf16[3,8,160,128]{3,2,0,1:T(8,128)(2,1)S(1)}, u32[]{:S(2)}, u32[]{:S(2)}) async-start(bf16[3,8,160,128]{3,2,0,1:T(8,128)(2,1)} %copy.22), calls=%async_computation | async-start | bytes 1966080 | tf_op jit(solution)/shard_map/all_to_all | solution.py:61
  18.4 0.7 dynamic-slice_bitcast_fusion
  19.0 36.1 %all-to-all-done = bf16[3,8,160,128]{3,2,0,1:T(8,128)(2,1)S(1)} async-done(((bf16[3,8,160,128]{3,2,0,1:T(8,128)(2,1)}), bf16[3,8,160,128]{3,2,0,1:T(8,128)(2,1)S(1)}, u32[]{:S(2)}, u32[]{:S(2)}) %all-to-all-start) | async-done | bytes 983072 | tf_op jit(solution)/shard_map/all_to_all | solution.py:61
  55.1 0.1 fusion.45
  55.1 1.3 multiply_reduce_fusion
  56.5 1.4 fusion
  57.8 0.0 copy-start
  57.9 1.8 fusion.25
  59.7 0.6 constant_dynamic-update-slice_fusion.7
  60.4 0.6 constant_dynamic-update-slice_fusion.6
  61.0 0.6 constant_dynamic-update-slice_fusion.5
  61.6 0.6 constant_dynamic-update-slice_fusion.4
  62.2 0.6 constant_dynamic-update-slice_fusion.3
  62.8 0.6 constant_dynamic-update-slice_fusion.2
  63.5 0.6 constant_dynamic-update-slice_fusion.1
  64.1 0.6 constant_dynamic-update-slice_fusion
  64.7 3.4 %all-to-all-start.1 = ((bf16[8,1,128,1,160]{2,4,3,1,0:T(8,128)(2,1)}), bf16[8,1,128,1,160]{2,4,3,1,0:T(8,128)(2,1)S(1)}, u32[]{:S(2)}, u32[]{:S(2)}) async-start(bf16[8,1,128,1,160]{2,4,3,1,0:T(8,128)(2,1)} %constant_dynamic-update-slice_fusion), calls=%async_computation.1 | async-start | bytes 655360 | tf_op jit(solution)/shard_map/all_to_all | solution.py:15
  68.1 0.0 all-gather.6.cloned.1.call-start
  68.2 0.1 fusion.43
  68.3 0.2 reduce_window_sum.11
  68.5 0.2 select_reduce_fusion
  68.6 0.7 multiply_add_fusion.1
  69.3 14.1 %all-to-all-done.1 = bf16[8,1,128,1,160]{2,4,3,1,0:T(8,128)(2,1)S(1)} async-done(((bf16[8,1,128,1,160]{2,4,3,1,0:T(8,128)(2,1)}), bf16[8,1,128,1,160]{2,4,3,1,0:T(8,128)(2,1)S(1)}, u32[]{:S(2)}, u32[]{:S(2)}) %all-to-all-start.1) | async-done | bytes 327712 | tf_op jit(solution)/shard_map/all_to_all | solution.py:15
  83.4 2.6 %fusion.47 = (f32[128]{0:T(128)S(1)}, f32[128,1280]{1,0:T(8,128)S(1)}) fusion(bf16[128,1280]{0,1:T(8,128)(2,1)S(1)} %bitcast.119, bf16[1280,1280]{1,0:T(8,128)(2,1)} %all-gather.4.cloned.1.call-done, bf16[1,128,1280]{2,1,0:T(8,128)(2,1)S(1)} %copy-done), kind=kOutput, calls=%fused_computation.73 | convolution fusion | flops 420249472 | bytes 4588032 | tf_op jit(solution)/shard_map/dot_general | solution.py:65
  86.1 0.2 multiply_reduce_fusion.1
  86.3 0.4 convolution_convert_fusion.2
  86.8 0.4 copy.30
  87.2 16.9 %all_to_all.20 = bf16[8,2,12,1280]{3,1,2,0:T(2,128)(2,1)} all-to-all(bf16[8,2,12,1280]{3,1,2,0:T(2,128)(2,1)S(1)} %copy.30), channel_id=1, replica_groups=mesh['seq'=8,'exp'=8,'img'=4] {'exp'}, dimensions={0} | all-to-all | bytes 983040 | tf_op jit(solution)/shard_map/all_to_all | solution.py:88
  104.1 0.0 all-gather.6.cloned.1.call-update
  104.1 0.2 reduce-scatter.2.cloned.1.call-start
  104.3 45.5 %all-gather.6.cloned.1.call-done = bf16[64,2,12,1280]{3,1,2,0:T(2,128)(2,1)} async-done(((bf16[8,2,12,1280]{3,1,2,0:T(2,128)(2,1)}), bf16[64,2,12,1280]{3,1,2,0:T(2,128)(2,1)}) %all-gather.6.cloned.1.call-update) | async-done | bytes 3932176 | tf_op jit(solution)/shard_map/all_gather | solution.py:89
  149.8 3.0 %copy.31 = bf16[64,2,12,1280]{3,2,0,1:T(8,128)(2,1)S(1)} copy(bf16[64,2,12,1280]{3,1,2,0:T(2,128)(2,1)} %all-gather.6.cloned.1.call-done) | data formatting | bytes 7864320 | tf_op jit(solution)/shard_map/all_gather | solution.py:89
  152.8 0.1 copy-done.3
  152.9 2.4 multiply_convert_fusion.3
  155.4 0.0 copy-start.4
  155.4 2.4 %multiply_convert_fusion.2 = bf16[8,8,12,640]{3,2,1,0:T(8,128)(2,1)S(1)} fusion(bf16[2,1280,640]{2,1,0:T(8,128)(2,1)S(1)} %copy-done.3, bf16[8,8,2,12,1280]{4,3,1,0,2:T(8,128)(2,1)S(1)} %bitcast.117), kind=kOutput, calls=%fused_computation.14 | convolution fusion | flops 1260748800 | bytes 5242880 | tf_op jit(solution)/shard_map/secd,df->secf/dot_general | solution.py:92
  157.8 2.2 fusion.2
  160.0 2.2 fusion.3
  162.2 0.7 pad_maximum_fusion
  163.0 3.4 %copy.32 = bf16[8,8,2,12,1280]{4,1,3,2,0:T(8,128)(2,1)} copy(bf16[8,8,2,12,1280]{4,3,1,0,2:T(8,128)(2,1)S(1)} %pad_maximum_fusion) | data formatting | bytes 7864320 | tf_op jit(solution)/shard_map/stack | solution.py:104
  166.4 0.0 reduce-scatter.2.cloned.1.call-update
  166.4 51.6 %reduce-scatter.2.cloned.1.call-done = bf16[1,8,2,12,1280]{4,1,3,2,0:T(8,128)(2,1)} async-done(((bf16[8,8,2,12,1280]{4,1,3,2,0:T(8,128)(2,1)}), bf16[1,8,2,12,1280]{4,1,3,2,0:T(8,128)(2,1)}) %reduce-scatter.2.cloned.1.call-update) | async-done | bytes 491536 | tf_op jit(solution)/shard_map/reduce_scatter | solution.py:105
  218.0 1.5 copy.33
  219.5 16.5 %all_to_all.21 = bf16[8,2,12,1280]{3,1,2,0:T(2,128)(2,1)S(1)} all-to-all(bf16[8,2,12,1280]{3,1,2,0:T(2,128)(2,1)S(1)} %copy.33), channel_id=1, replica_groups=mesh['seq'=8,'exp'=8,'img'=4] {'exp'}, dimensions={0} | all-to-all | bytes 983040 | tf_op jit(solution)/shard_map/all_to_all | solution.py:106
  236.0 1.1 fusion.10
  (14 shorter events, 0.1 us)
Async XLA Ops:
  6.5 76.9 %all-gather.4.cloned.1.call-start = ((), (), s32[]{:S(2)}) async-start(), calls=%async_computation.5 | async-start | bytes 3686400 | tf_op jit(solution)/shard_map/all_gather | solution.py:67
  9.9 45.2 %all-to-all-start = ((bf16[3,8,160,128]{3,2,0,1:T(8,128)(2,1)}), bf16[3,8,160,128]{3,2,0,1:T(8,128)(2,1)S(1)}, u32[]{:S(2)}, u32[]{:S(2)}) async-start(bf16[3,8,160,128]{3,2,0,1:T(8,128)(2,1)} %copy.22), calls=%async_computation | async-start | bytes 1966080 | tf_op jit(solution)/shard_map/all_to_all | solution.py:61
  57.8 25.6 %copy-start = (bf16[1,128,1280]{2,1,0:T(8,128)(2,1)S(1)}, bf16[1,128,1280]{2,1,0:T(8,128)(2,1)}, u32[]{:S(2)}) copy-start(bf16[1,128,1280]{2,1,0:T(8,128)(2,1)} %param.9) | copy-start | bytes 983044
  62.2 24.1 %copy-start.1 = (f32[1280]{0:T(1024)S(1)}, f32[1280]{0:T(1024)}, u32[]{:S(2)}) copy-start(f32[1280]{0:T(1024)} %param.12) | copy-start | bytes 15364
  62.2 24.1 %copy-start.2 = (f32[1280]{0:T(1024)S(1)}, f32[1280]{0:T(1024)}, u32[]{:S(2)}) copy-start(f32[1280]{0:T(1024)} %param.11) | copy-start | bytes 15364
  64.7 18.7 %all-to-all-start.1 = ((bf16[8,1,128,1,160]{2,4,3,1,0:T(8,128)(2,1)}), bf16[8,1,128,1,160]{2,4,3,1,0:T(8,128)(2,1)S(1)}, u32[]{:S(2)}, u32[]{:S(2)}) async-start(bf16[8,1,128,1,160]{2,4,3,1,0:T(8,128)(2,1)} %constant_dynamic-update-slice_fusion), calls=%async_computation.1 | async-start | bytes 655360 | tf_op jit(solution)/shard_map/all_to_all | solution.py:15
  68.1 81.7 %all-gather.6.cloned.1.call-start = ((), (), s32[]{:S(2)}) async-start(), calls=%async_computation.7 | async-start | bytes 4423680 | tf_op jit(solution)/shard_map/all_gather | solution.py:89
  104.1 113.9 %reduce-scatter.2.cloned.1.call-start = ((), (), s32[]{:S(2)}) async-start(), calls=%async_computation.6 | async-start | bytes 4423680 | tf_op jit(solution)/shard_map/reduce_scatter | solution.py:105
  149.8 3.1 %copy-start.3 = (bf16[2,1280,640]{2,1,0:T(8,128)(2,1)S(1)}, bf16[2,1280,640]{2,1,0:T(8,128)(2,1)}, u32[]{:S(2)}) copy-start(bf16[2,1280,640]{2,1,0:T(8,128)(2,1)} %param.14) | copy-start | bytes 9830404
  155.4 2.5 %copy-start.4 = (bf16[2,640,1280]{2,1,0:T(8,128)(2,1)S(1)}, bf16[2,640,1280]{2,1,0:T(8,128)(2,1)}, u32[]{:S(2)}) copy-start(bf16[2,640,1280]{2,1,0:T(8,128)(2,1)} %param.15) | copy-start | bytes 9830404
Sparse Core Ops, SparseCore 0:
  9.1 68.4 all-gather.3
  104.2 45.5 all-gather.5
  166.5 51.4 reduce-scatter.1
